TPU v7x, 512 devices: a whole 4x8x8 slice. The times are simulated.
512 devices in a mesh: blk: 64 (over y_lo, z, core), tp: 8 (over y_hi, x).
Axes of the slice: x: 4, y: 8 (y_hi: 2, y_lo: 4; y = y_hi * 4 + y_lo), z: 8, core: 2. Of those that a mesh axis runs over, the one named last changes fastest.
Arguments:
- embeds: bfloat16 [8192, 5120], P('blk', 'tp')
- given_embeds: bfloat16 [8192, 5120], P('blk', 'tp')
- accept: int32 [8192], P('blk'), may hold values 0 or 1
- lengths: int32 [64], P('blk'), may hold values from 4 to 4096, as said below
- block_keep: int32 [64, 64], P('blk'), may hold values from 0 to 1
- norm_gain: bfloat16 [5120], replicated, may hold values from 0.25 to 1.75
- w_query: bfloat16 [5120, 5120], P('blk', 'tp'), may hold values from -0.078125 to 0.078125
- b_query: bfloat16 [5120], P('tp'), may hold values from -4 to 4
- w_key: bfloat16 [5120, 1024], P('blk', 'tp'), may hold values from -0.078125 to 0.078125
- b_key: bfloat16 [1024], P('tp'), may hold values from -4 to 4
- w_value: bfloat16 [5120, 1024], P('blk', 'tp'), may hold values from -0.078125 to 0.078125
- b_value: bfloat16 [1024], P('tp'), may hold values from -4 to 4
- cache_keys: bfloat16 [4096, 1024], P('blk', 'tp'), as said below
- cache_values: bfloat16 [4096, 1024], P('blk', 'tp'), may hold values from -6 to 6
Outputs:
- first_pass: bfloat16 [8192, 5120], P('blk', 'tp')
- second_pass: bfloat16 [8192, 5120], P('blk', 'tp')
Inputs may be any that keep to these rules, and one draw needn't show every extreme that they name: `lengths`: every request sees at least the first 4 prompt positions; some request sees all 4096. `cache_keys`: entries lie between -160 and 160.
All inputs are finite; a program needn't handle non-finite values. No bound on the sum of `accept` on one device may be relied on, other than what follows from the above.
Results may differ from a plain program's by a relative error of at most 0.012.
The roundings to bfloat16 on the way count: a program that leaves them out, or rounds other values in their place, can miss the bound.
Values may be sent and summed in bfloat16 or wider, within the bound.
No kernel may reach another device: no remote copies, remote signals or barrier semaphores. Data moves between devices by JAX's collectives and lax.ppermute only.
A program may use at most 64 MiB of HBM per device.

v0:
```python
import math
import jax
import jax.numpy as jnp
from jax import lax
from jax.sharding import PartitionSpec as P

KVH = 8
HD = 128
HQ = 40
CB = 64


def rotate(vectors, positions):
    halfway = HD // 2
    frequency = 1000000.0 ** (-(jnp.arange(halfway, dtype=jnp.float32) * (2.0 / HD)))
    angles = positions[..., None] * frequency
    cosine = jnp.cos(angles)[..., None, :]
    sine_part = jnp.sin(angles)[..., None, :]
    front_part = vectors[..., :halfway]
    back_part = vectors[..., halfway:]
    return jnp.concatenate(
        [front_part * cosine - back_part * sine_part, back_part * cosine + front_part * sine_part],
        axis=-1,
    )


def normalize(rows_in, norm_gain):
    widened = rows_in.astype(jnp.float32)
    inverse = lax.rsqrt(jnp.mean(widened * widened, axis=-1, keepdims=True) + 1e-06)
    return (widened * inverse * norm_gain.astype(jnp.float32)).astype(jnp.bfloat16)


def local(
    embeds,
    given_embeds,
    accept,
    lengths,
    block_keep,
    norm_gain,
    w_query,
    b_query,
    w_key,
    b_key,
    w_value,
    b_value,
    cache_keys,
    cache_values,
):
    grouping = HQ // KVH
    local_kv = w_key.shape[1] // HD
    local_q = local_kv * grouping
    block_rows = embeds.shape[0]
    blocks_all = block_keep.shape[1]
    inv_root = 1.0 / math.sqrt(HD)
    first_rows, given_rows = (
        lax.all_gather(embeds, "tp", axis=1, tiled=True),
        lax.all_gather(given_embeds, "tp", axis=1, tiled=True),
    )
    revised = jnp.where(accept[:, None] == 1, given_rows, first_rows)
    normed = normalize(jnp.concatenate([first_rows, revised], axis=0), norm_gain)
    pieces = (
        lax.all_gather(w_query, "blk", axis=0, tiled=True),
        lax.all_gather(w_key, "blk", axis=0, tiled=True),
        lax.all_gather(w_value, "blk", axis=0, tiled=True),
    )
    queries, key_proj, value_proj = tuple(
        (
            jnp.dot(normed, weight_piece, preferred_element_type=jnp.float32)
            for weight_piece in pieces
        )
    )
    queries = queries + b_query.astype(jnp.float32)
    key_proj = key_proj + b_key.astype(jnp.float32)
    value_proj = value_proj + b_value.astype(jnp.float32)
    length = lengths[0]
    keep_row = block_keep[0]
    positions = length.astype(jnp.float32) + jnp.arange(block_rows, dtype=jnp.float32)
    q_rot = rotate(queries.reshape(2, block_rows, local_q, HD), positions).astype(jnp.bfloat16)
    q_rot = q_rot.reshape(2, block_rows, local_kv, grouping, HD)
    k_rot = rotate(key_proj.reshape(2, block_rows, local_kv, HD), positions).astype(jnp.bfloat16)
    value_rows = value_proj.astype(jnp.bfloat16).reshape(2, block_rows, local_kv, HD)
    own_scores = (
        jnp.einsum("pqkgd,pjkd->pkgqj", q_rot, k_rot, preferred_element_type=jnp.float32) * inv_root
    )
    highest = jnp.max(own_scores, axis=-1)
    own_weights = jnp.exp(own_scores - highest[..., None])
    totals = jnp.sum(own_weights, axis=-1)
    mixture = jnp.einsum(
        "pkgqj,pjkd->pkgqd",
        own_weights.astype(jnp.bfloat16),
        value_rows,
        preferred_element_type=jnp.float32,
    )
    running = (highest, totals, mixture)
    key_piece = lax.all_gather(cache_keys, "blk", axis=0, tiled=True)
    value_piece = lax.all_gather(cache_values, "blk", axis=0, tiled=True)
    piece_rows = key_piece.shape[0]
    sub_rows = math.gcd(piece_rows, CB)
    count = piece_rows // sub_rows
    key_blocks = key_piece.reshape(count, sub_rows, local_kv, HD)
    value_blocks = value_piece.reshape(count, sub_rows, local_kv, HD)
    block_starts = jnp.arange(count, dtype=jnp.int32) * sub_rows

    def visit(running_now, inputs):
        key_rows, value_block, position = inputs
        cache_index = position + jnp.arange(sub_rows, dtype=jnp.int32)
        block_index = cache_index // CB
        matches = block_index[:, None] == jnp.arange(blocks_all, dtype=jnp.int32)[None, :]
        kept = jnp.sum(jnp.where(matches, keep_row[None, :], 0), axis=1)
        visible = (cache_index < length) & (kept == 1)
        best_old, sums_old, mixed_old = running_now
        scores = (
            jnp.einsum("pqkgd,ckd->pkgqc", q_rot, key_rows, preferred_element_type=jnp.float32)
            * inv_root
        )
        scores = jnp.where(visible, scores, -jnp.inf)
        best_new = jnp.maximum(best_old, jnp.max(scores, axis=-1))
        weights = jnp.where(visible, jnp.exp(scores - best_new[..., None]), 0.0)
        factor = jnp.exp(best_old - best_new)
        sums_new = sums_old * factor + jnp.sum(weights, axis=-1)
        mixed_new = mixed_old * factor[..., None] + jnp.einsum(
            "pkgqc,ckd->pkgqd",
            weights.astype(jnp.bfloat16),
            value_block,
            preferred_element_type=jnp.float32,
        )
        return ((best_new, sums_new, mixed_new), None)

    result, ignored = lax.scan(visit, running, (key_blocks, value_blocks, block_starts))
    running = result
    highest, totals, mixture = running
    attended = mixture / totals[..., None]
    attended = (
        jnp.transpose(attended, (0, 3, 1, 2, 4))
        .reshape(2 * block_rows, local_q * HD)
        .astype(jnp.bfloat16)
    )
    return (attended[:block_rows], attended[block_rows:])


def solution(mesh):
    return jax.shard_map(
        local,
        mesh=mesh,
        in_specs=(
            P("blk", "tp"),
            P("blk", "tp"),
            P("blk"),
            P("blk"),
            P("blk", None),
            P(),
            P("blk", "tp"),
            P("tp"),
            P("blk", "tp"),
            P("tp"),
            P("blk", "tp"),
            P("tp"),
            P("blk", "tp"),
            P("blk", "tp"),
        ),
        out_specs=(P("blk", "tp"), P("blk", "tp")),
        check_vma=False,
    )
```

profile of v0, /device:TPU:59, one launch (start us, length us, event | category | flops | bytes accessed | tf_op | source)
XLA Modules:
  0.0 1078.7 jit_solution(2611596930218597881)
XLA Ops:
  16.3 62.3 %all-gather.8.cloned.1.call-done = bf16[128,5120]{1,0:T(8,128)(2,1)} async-done(((bf16[128,640]{1,0:T(8,128)(2,1)}), bf16[128,5120]{1,0:T(8,128)(2,1)}) %all-gather.8.cloned.1.call-update) | async-done | bytes 1310736 | tf_op jit(solution)/shard_map/all_gather | solution.py:56
  78.6 69.6 %all-gather.10.cloned.1.call-done = bf16[128,5120]{1,0:T(8,128)(2,1)} async-done(((bf16[128,640]{1,0:T(8,128)(2,1)}), bf16[128,5120]{1,0:T(8,128)(2,1)}) %all-gather.10.cloned.1.call-update) | async-done | bytes 1310736 | tf_op jit(solution)/shard_map/all_gather | solution.py:57
  148.2 1.9 broadcast_select_fusion
  150.8 121.0 %all-gather.12.cloned.1.call-done = bf16[5120,128]{1,0:T(8,128)(2,1)} async-done(((bf16[80,128]{1,0:T(8,128)(2,1)}), bf16[5120,128]{1,0:T(8,128)(2,1)}) %all-gather.12.cloned.1.call-update) | async-done | bytes 1310736 | tf_op jit(solution)/shard_map/all_gather | solution.py:63
  271.8 2.3 convolution_add_fusion.2
  274.2 115.1 %all-gather.16.cloned.1.call-done = bf16[5120,128]{1,0:T(8,128)(2,1)} async-done(((bf16[80,128]{1,0:T(8,128)(2,1)}), bf16[5120,128]{1,0:T(8,128)(2,1)}) %all-gather.16.cloned.1.call-update) | async-done | bytes 1310736 | tf_op jit(solution)/shard_map/all_gather | solution.py:64
  389.3 2.9 fusion.24
  392.2 120.2 %all-gather.14.cloned.1.call-done = bf16[5120,640]{1,0:T(8,128)(2,1)} async-done(((bf16[80,640]{1,0:T(8,128)(2,1)}), bf16[5120,640]{1,0:T(8,128)(2,1)}) %all-gather.14.cloned.1.call-update) | async-done | bytes 6553616 | tf_op jit(solution)/shard_map/all_gather | solution.py:62
  512.4 5.1 convolution_add_fusion
  519.3 109.8 %all-gather.18.cloned.1.call-done = bf16[4096,128]{1,0:T(8,128)(2,1)} async-done(((bf16[64,128]{1,0:T(8,128)(2,1)}), bf16[4096,128]{1,0:T(8,128)(2,1)}) %all-gather.18.cloned.1.call-update) | async-done | bytes 1048592 | tf_op jit(solution)/shard_map/all_gather | solution.py:95
  629.1 116.8 %all-gather.20.cloned.1.call-done = bf16[4096,128]{1,0:T(8,128)(2,1)} async-done(((bf16[64,128]{1,0:T(8,128)(2,1)}), bf16[4096,128]{1,0:T(8,128)(2,1)}) %all-gather.20.cloned.1.call-update) | async-done | bytes 1048592 | tf_op jit(solution)/shard_map/all_gather | solution.py:96
  745.8 324.3 %while.16 = (s32[]{:T(128)}, f32[2,1,5,128]{3,2,0,1:T(8,128)S(1)}, f32[2,1,5,128]{3,2,0,1:T(8,128)S(1)}, f32[2,1,5,128,128]{3,4,2,0,1:T(8,128)S(1)}, s32[64]{0:T...) while((s32[]{:T(128)}, f32[2,1,5,128]{3,2,0,1:T(8,128)S(1)}, ...), condition=%wide.region_7.8_spmd, body=%wide.region_3.7_spmd.sunk | while | flops 43025344 | bytes 2738821 | solution.py:129
  747.3 1.3 compare_and_fusion.2
  752.3 1.3 compare_and_fusion.2
  757.4 1.3 compare_and_fusion.2
  762.5 1.3 compare_and_fusion.2
  767.5 1.3 compare_and_fusion.2
  772.6 1.3 compare_and_fusion.2
  777.7 1.3 compare_and_fusion.2
  782.7 1.3 compare_and_fusion.2
  787.8 1.3 compare_and_fusion.2
  792.9 1.3 compare_and_fusion.2
  797.9 1.3 compare_and_fusion.2
  803.0 1.3 compare_and_fusion.2
  808.1 1.3 compare_and_fusion.2
  813.1 1.3 compare_and_fusion.2
  818.2 1.3 compare_and_fusion.2
  823.3 1.3 compare_and_fusion.2
  828.3 1.3 compare_and_fusion.2
  833.4 1.3 compare_and_fusion.2
  838.5 1.3 compare_and_fusion.2
  843.5 1.3 compare_and_fusion.2
  848.6 1.3 compare_and_fusion.2
  853.7 1.3 compare_and_fusion.2
  858.7 1.3 compare_and_fusion.2
  863.8 1.3 compare_and_fusion.2
  868.9 1.3 compare_and_fusion.2
  874.0 1.3 compare_and_fusion.2
  879.0 1.3 compare_and_fusion.2
  884.1 1.3 compare_and_fusion.2
  889.2 1.3 compare_and_fusion.2
  894.2 1.3 compare_and_fusion.2
  899.3 1.3 compare_and_fusion.2
  904.4 1.3 compare_and_fusion.2
  909.4 1.3 compare_and_fusion.2
  914.5 1.3 compare_and_fusion.2
  919.6 1.3 compare_and_fusion.2
  924.6 1.3 compare_and_fusion.2
  929.7 1.3 compare_and_fusion.2
  934.8 1.3 compare_and_fusion.2
  939.8 1.3 compare_and_fusion.2
  944.9 1.3 compare_and_fusion.2
  950.0 1.3 compare_and_fusion.2
  955.0 1.3 compare_and_fusion.2
  960.1 1.3 compare_and_fusion.2
  965.2 1.3 compare_and_fusion.2
  970.2 1.3 compare_and_fusion.2
  975.3 1.3 compare_and_fusion.2
  980.4 1.3 compare_and_fusion.2
  985.4 1.3 compare_and_fusion.2
  990.5 1.3 compare_and_fusion.2
  995.6 1.3 compare_and_fusion.2
  1000.6 1.3 compare_and_fusion.2
  1020.9 1.3 compare_and_fusion.2
  (633 shorter events, 264.4 us)
Async XLA Ops:
  7.2 71.4 %all-gather.8.cloned.1.call-start = ((), (), s32[]{:S(2)}) async-start(), calls=%async_computation | async-start | bytes 1474560 | tf_op jit(solution)/shard_map/all_gather | solution.py:56
  7.9 140.3 %all-gather.10.cloned.1.call-start = ((), (), s32[]{:S(2)}) async-start(), calls=%async_computation.1 | async-start | bytes 1474560 | tf_op jit(solution)/shard_map/all_gather | solution.py:57
  8.6 263.1 %all-gather.12.cloned.1.call-start = ((), (), s32[]{:S(2)}) async-start(), calls=%async_computation.2 | async-start | bytes 1331200 | tf_op jit(solution)/shard_map/all_gather | solution.py:63
  9.4 379.9 %all-gather.16.cloned.1.call-start = ((), (), s32[]{:S(2)}) async-start(), calls=%async_computation.4 | async-start | bytes 1331200 | tf_op jit(solution)/shard_map/all_gather | solution.py:64
  10.0 502.5 %all-gather.14.cloned.1.call-start = ((), (), s32[]{:S(2)}) async-start(), calls=%async_computation.3 | async-start | bytes 6656000 | tf_op jit(solution)/shard_map/all_gather | solution.py:62
  10.5 618.5 %all-gather.18.cloned.1.call-start = ((), (), s32[]{:S(2)}) async-start(), calls=%async_computation.5 | async-start | bytes 1064960 | tf_op jit(solution)/shard_map/all_gather | solution.py:95
  11.1 734.7 %all-gather.20.cloned.1.call-start = ((), (), s32[]{:S(2)}) async-start(), calls=%async_computation.6 | async-start | bytes 1064960 | tf_op jit(solution)/shard_map/all_gather | solution.py:96
  13.3 376.0 %copy-start.2 = (f32[5120]{0:T(1024)}, f32[5120]{0:T(1024)S(1)}, u32[]{:S(2)}) copy-start(f32[5120]{0:T(1024)S(1)} %convert_element_type.54) | copy-start | bytes 61444
  78.6 71.6 %copy-start = (bf16[128,5120]{1,0:T(8,128)(2,1)S(1)}, bf16[128,5120]{1,0:T(8,128)(2,1)}, u32[]{:S(2)}) copy-start(bf16[128,5120]{1,0:T(8,128)(2,1)} %all-gather.8.cloned.1.call-done) | copy-start | bytes 3932164
  518.0 1.0 copy-start.1
  518.3 227.6 %copy-start.3 = (s32[1,64]{1,0:T(1,128)S(1)}, s32[1,64]{1,0:T(1,128)}, u32[]{:S(2)}) copy-start(s32[1,64]{1,0:T(1,128)} %param.20) | copy-start | bytes 772
Sparse Core Ops, SparseCore 0:
  11.2 67.3 all-gather.7
  81.8 66.3 all-gather.9
  150.4 121.3 all-gather.11
  273.8 115.4 all-gather.15
  391.3 121.0 all-gather.13
  514.4 114.6 all-gather.17
  631.2 114.5 all-gather.19
where the time goes:
time: 1090 us; the launch traced here: 1080 us
  waiting for transfers between devices  719 us (66%)
  other arithmetic  152 us (14%)
  matrix products  149 us (14%)
  local copies, waits for them, and re-layouts  39.8 us (4%)
  between operations  14.9 us (1%)
    all_gather x1, waiting for transfers between devices, local(): lax.all_gather(w_key, 'blk', axis=0, tiled=True)  121 us
    all_gather x1, waiting for transfers between devices, local(): lax.all_gather(w_query, 'blk', axis=0, tiled=True)  120 us
    all_gather x1, waiting for transfers between devices, local(): value_piece = lax.all_gather(cache_values, 'blk', axis=0, tiled=True)  117 us
    all_gather x1, waiting for transfers between devices, local(): lax.all_gather(w_value, 'blk', axis=0, tiled=True)  115 us
    all_gather x1, waiting for transfers between devices, local(): key_piece = lax.all_gather(cache_keys, 'blk', axis=0, tiled=True)  110 us
    and x64, other arithmetic, visit(): visible = (cache_index < length) & (kept == 1)  83.6 us
    dot_general x64, matrix products, visit(): jnp.einsum('pkgqc,ckd->pkgqd', weights.astype(jnp.bfloat16), value_block,...  75.1 us
    all_gather x1, waiting for transfers between devices, local(): lax.all_gather(given_embeds, 'tp', axis=1, tiled=True)  69.6 us
  transfers between devices with their start and end apart: 7, of which 7 were waited for; matrix products, arithmetic and copies ran while one was open for 2% of the time, Pallas kernels for 0%

commit v1 on v0

--- a/solution.py
+++ b/solution.py
@@ -3,6 +3,7 @@
 import jax.numpy as jnp
 from jax import lax
 from jax.sharding import PartitionSpec as P
+from jax.lax import all_to_all, axis_size
 
 KVH = 8
 HD = 128
@@ -52,8 +53,11 @@
     block_rows = embeds.shape[0]
     blocks_all = block_keep.shape[1]
     inv_root = 1.0 / math.sqrt(HD)
+    write_orders = lambda t0: jnp.concatenate(
+        all_to_all(jnp.stack([t0 for _ in range(axis_size("tp"))], axis=0), "tp", 0, 0), 1
+    )
     first_rows, given_rows = (
-        lax.all_gather(embeds, "tp", axis=1, tiled=True),
+        write_orders(embeds),
         lax.all_gather(given_embeds, "tp", axis=1, tiled=True),
     )
     revised = jnp.where(accept[:, None] == 1, given_rows, first_rows)

time: 1090 us -> 1040 us (0.954)
  waiting for transfers between devices: 719 us -> 654 us
    all_gather x1 -> x0, waiting for transfers between devices: 62.3 us -> none  [local(): lax.all_gather(embeds, 'tp', axis=1, tiled=True)]
    all_gather x1, waiting for transfers between devices: 69.6 us -> 52.6 us  [local(): lax.all_gather(given_embeds, 'tp', axis=1, tiled=True)]
    all_to_all x0 -> x1, waiting for transfers between devices: none -> 16.9 us  [local(): all_to_all(jnp.stack([t0 for _ in range(axis_size('tp'))], axis=0), 'tp',...]
where the time goes in v1:
time: 1040 us; the launch traced here: 1030 us
  waiting for transfers between devices  654 us (63%)
  matrix products  151 us (15%)
  other arithmetic  148 us (14%)
  local copies, waits for them, and re-layouts  44.4 us (4%)
  between operations  15 us (1%)
    all_gather x1, waiting for transfers between devices, local(): lax.all_gather(w_key, 'blk', axis=0, tiled=True)  121 us
    all_gather x1, waiting for transfers between devices, local(): lax.all_gather(w_query, 'blk', axis=0, tiled=True)  120 us
    all_gather x1, waiting for transfers between devices, local(): value_piece = lax.all_gather(cache_values, 'blk', axis=0, tiled=True)  117 us
    all_gather x1, waiting for transfers between devices, local(): lax.all_gather(w_value, 'blk', axis=0, tiled=True)  115 us
    all_gather x1, waiting for transfers between devices, local(): key_piece = lax.all_gather(cache_keys, 'blk', axis=0, tiled=True)  109 us
    and x64, other arithmetic, visit(): visible = (cache_index < length) & (kept == 1)  83.6 us
    dot_general x64, matrix products, visit(): jnp.einsum('pkgqc,ckd->pkgqd', weights.astype(jnp.bfloat16), value_block,...  75.1 us
    dot_general x64, matrix products, visit(): jnp.einsum('pqkgd,ckd->pkgqc', q_rot, key_rows, preferred_element_type=jn...  62.6 us
  transfers between devices with their start and end apart: 7, of which 7 were waited for; matrix products, arithmetic and copies ran while one was open for 2% of the time, Pallas kernels for 0%

profile of v1, /device:TPU:59, one launch (start us, length us, event | category | flops | bytes accessed | tf_op | source)
XLA Modules:
  0.0 1025.4 jit_solution(9416742520710609554)
XLA Ops:
  7.3 1.7 copy.49
  11.7 2.1 stack.2
  13.7 9.1 all-to-all-start
  24.5 16.9 %all-to-all-done = bf16[8,128,640]{2,1,0:T(8,128)(2,1)S(1)} async-done(((bf16[8,128,640]{2,1,0:T(8,128)(2,1)}), bf16[8,128,640]{2,1,0:T(8,128)(2,1)S(1)}, u32[]{:S(2)}, u32[]{:S(2)}) %all-to-all-start) | async-done | bytes 1310752 | tf_op jit(solution)/shard_map/all_to_all | solution.py:57
  42.2 52.6 %all-gather.7.cloned.1.call-done = bf16[128,5120]{0,1:T(8,128)(2,1)} async-done(((bf16[128,640]{0,1:T(8,128)(2,1)}), bf16[128,5120]{0,1:T(8,128)(2,1)}) %all-gather.7.cloned.1.call-update) | async-done | bytes 1310736 | tf_op jit(solution)/shard_map/all_gather | solution.py:61
  94.8 1.5 broadcast_select_fusion
  97.0 121.4 %all-gather.9.cloned.1.call-done = bf16[5120,128]{1,0:T(8,128)(2,1)} async-done(((bf16[80,128]{1,0:T(8,128)(2,1)}), bf16[5120,128]{1,0:T(8,128)(2,1)}) %all-gather.9.cloned.1.call-update) | async-done | bytes 1310736 | tf_op jit(solution)/shard_map/all_gather | solution.py:67
  218.4 3.0 convolution_add_fusion.2
  221.5 114.6 %all-gather.13.cloned.1.call-done = bf16[5120,128]{1,0:T(8,128)(2,1)} async-done(((bf16[80,128]{1,0:T(8,128)(2,1)}), bf16[5120,128]{1,0:T(8,128)(2,1)}) %all-gather.13.cloned.1.call-update) | async-done | bytes 1310736 | tf_op jit(solution)/shard_map/all_gather | solution.py:68
  336.0 3.6 fusion.24
  339.6 119.5 %all-gather.11.cloned.1.call-done = bf16[5120,640]{1,0:T(8,128)(2,1)} async-done(((bf16[80,640]{1,0:T(8,128)(2,1)}), bf16[5120,640]{1,0:T(8,128)(2,1)}) %all-gather.11.cloned.1.call-update) | async-done | bytes 6553616 | tf_op jit(solution)/shard_map/all_gather | solution.py:66
  459.2 5.6 convolution_add_fusion
  466.5 109.3 %all-gather.15.cloned.1.call-done = bf16[4096,128]{1,0:T(8,128)(2,1)} async-done(((bf16[64,128]{1,0:T(8,128)(2,1)}), bf16[4096,128]{1,0:T(8,128)(2,1)}) %all-gather.15.cloned.1.call-update) | async-done | bytes 1048592 | tf_op jit(solution)/shard_map/all_gather | solution.py:99
  575.8 116.6 %all-gather.17.cloned.1.call-done = bf16[4096,128]{1,0:T(8,128)(2,1)} async-done(((bf16[64,128]{1,0:T(8,128)(2,1)}), bf16[4096,128]{1,0:T(8,128)(2,1)}) %all-gather.17.cloned.1.call-update) | async-done | bytes 1048592 | tf_op jit(solution)/shard_map/all_gather | solution.py:100
  692.4 324.4 %while.16 = (s32[]{:T(128)}, f32[2,1,5,128]{3,2,0,1:T(8,128)S(1)}, f32[2,1,5,128]{3,2,0,1:T(8,128)S(1)}, f32[2,1,5,128,128]{3,4,2,0,1:T(8,128)S(1)}, s32[64]{0:T...) while((s32[]{:T(128)}, f32[2,1,5,128]{3,2,0,1:T(8,128)S(1)}, ...), condition=%wide.region_7.8_spmd, body=%wide.region_3.7_spmd.sunk | while | flops 43025344 | bytes 2738821 | solution.py:133
  693.9 1.3 compare_and_fusion.2
  698.9 1.3 compare_and_fusion.2
  704.0 1.3 compare_and_fusion.2
  709.1 1.3 compare_and_fusion.2
  714.1 1.3 compare_and_fusion.2
  719.2 1.3 compare_and_fusion.2
  724.3 1.3 compare_and_fusion.2
  729.3 1.3 compare_and_fusion.2
  734.4 1.3 compare_and_fusion.2
  739.5 1.3 compare_and_fusion.2
  744.5 1.3 compare_and_fusion.2
  749.6 1.3 compare_and_fusion.2
  754.7 1.3 compare_and_fusion.2
  759.8 1.3 compare_and_fusion.2
  764.8 1.3 compare_and_fusion.2
  769.9 1.3 compare_and_fusion.2
  775.0 1.3 compare_and_fusion.2
  780.0 1.3 compare_and_fusion.2
  785.1 1.3 compare_and_fusion.2
  790.2 1.3 compare_and_fusion.2
  795.2 1.3 compare_and_fusion.2
  800.3 1.3 compare_and_fusion.2
  805.4 1.3 compare_and_fusion.2
  810.4 1.3 compare_and_fusion.2
  815.5 1.3 compare_and_fusion.2
  820.6 1.3 compare_and_fusion.2
  825.6 1.3 compare_and_fusion.2
  830.7 1.3 compare_and_fusion.2
  835.8 1.3 compare_and_fusion.2
  840.8 1.3 compare_and_fusion.2
  845.9 1.3 compare_and_fusion.2
  851.0 1.3 compare_and_fusion.2
  856.1 1.3 compare_and_fusion.2
  861.1 1.3 compare_and_fusion.2
  866.2 1.3 compare_and_fusion.2
  871.3 1.3 compare_and_fusion.2
  876.3 1.3 compare_and_fusion.2
  881.4 1.3 compare_and_fusion.2
  886.5 1.3 compare_and_fusion.2
  891.5 1.3 compare_and_fusion.2
  896.6 1.3 compare_and_fusion.2
  901.7 1.3 compare_and_fusion.2
  906.7 1.3 compare_and_fusion.2
  911.8 1.3 compare_and_fusion.2
  916.9 1.3 compare_and_fusion.2
  921.9 1.3 compare_and_fusion.2
  927.0 1.3 compare_and_fusion.2
  932.1 1.3 compare_and_fusion.2
  962.5 1.3 compare_and_fusion.2
  (643 shorter events, 264.6 us)
Async XLA Ops:
  7.2 16.2 %copy-start.2 = (bf16[5120]{0:T(1024)(128)(2,1)S(1)}, bf16[5120]{0:T(1024)(128)(2,1)}, u32[]{:S(2)}) copy-start(bf16[5120]{0:T(1024)(128)(2,1)} %param.21) | copy-start | bytes 30724
  7.2 16.2 %copy-start.3 = (bf16[640]{0:T(1024)(128)(2,1)S(1)}, bf16[640]{0:T(1024)(128)(2,1)}, u32[]{:S(2)}) copy-start(bf16[640]{0:T(1024)(128)(2,1)} %param.23) | copy-start | bytes 3844
  7.2 16.9 %copy-start.4 = (bf16[128]{0:T(256)(128)(2,1)S(1)}, bf16[128]{0:T(256)(128)(2,1)}, u32[]{:S(2)}) copy-start(bf16[128]{0:T(256)(128)(2,1)} %param.25) | copy-start | bytes 772
  7.2 16.9 %copy-start.5 = (bf16[128]{0:T(256)(128)(2,1)S(1)}, bf16[128]{0:T(256)(128)(2,1)}, u32[]{:S(2)}) copy-start(bf16[128]{0:T(256)(128)(2,1)} %param.27) | copy-start | bytes 772
  7.2 17.0 %copy-start.6 = (s32[128]{0:T(128)S(1)}, s32[128]{0:T(128)}, u32[]{:S(2)}) copy-start(s32[128]{0:T(128)} %param.18) | copy-start | bytes 1540
  7.2 87.6 %all-gather.7.cloned.1.call-start = ((), (), s32[]{:S(2)}) async-start(), calls=%async_computation.1 | async-start | bytes 1474560 | tf_op jit(solution)/shard_map/all_gather | solution.py:61
  9.0 209.4 %all-gather.9.cloned.1.call-start = ((), (), s32[]{:S(2)}) async-start(), calls=%async_computation.2 | async-start | bytes 1331200 | tf_op jit(solution)/shard_map/all_gather | solution.py:67
  9.8 326.3 %all-gather.13.cloned.1.call-start = ((), (), s32[]{:S(2)}) async-start(), calls=%async_computation.4 | async-start | bytes 1331200 | tf_op jit(solution)/shard_map/all_gather | solution.py:68
  10.5 448.7 %all-gather.11.cloned.1.call-start = ((), (), s32[]{:S(2)}) async-start(), calls=%async_computation.3 | async-start | bytes 6656000 | tf_op jit(solution)/shard_map/all_gather | solution.py:66
  11.1 564.7 %all-gather.15.cloned.1.call-start = ((), (), s32[]{:S(2)}) async-start(), calls=%async_computation.5 | async-start | bytes 1064960 | tf_op jit(solution)/shard_map/all_gather | solution.py:99
  13.7 27.7 %all-to-all-start = ((bf16[8,128,640]{2,1,0:T(8,128)(2,1)}), bf16[8,128,640]{2,1,0:T(8,128)(2,1)S(1)}, u32[]{:S(2)}, u32[]{:S(2)}) async-start(bf16[8,128,640]{2,1,0:T(8,128)(2,1)} %stack.2), calls=%async_computation | async-start | bytes 2621440 | tf_op jit(solution)/shard_map/all_to_all | solution.py:57
  22.8 669.6 %all-gather.17.cloned.1.call-start = ((), (), s32[]{:S(2)}) async-start(), calls=%async_computation.6 | async-start | bytes 1064960 | tf_op jit(solution)/shard_map/all_gather | solution.py:100
  23.4 312.6 %copy-start.1 = (f32[5120]{0:T(1024)}, f32[5120]{0:T(1024)S(1)}, u32[]{:S(2)}) copy-start(f32[5120]{0:T(1024)S(1)} %convert_element_type.54) | copy-start | bytes 61444
  465.2 1.0 copy-start
  465.5 226.9 %copy-start.7 = (s32[1,64]{1,0:T(1,128)S(1)}, s32[1,64]{1,0:T(1,128)}, u32[]{:S(2)}) copy-start(s32[1,64]{1,0:T(1,128)} %param.20) | copy-start | bytes 772
Sparse Core Ops, SparseCore 0:
  11.8 82.9 all-gather.6
  96.9 121.3 all-gather.8
  220.5 115.4 all-gather.12
  338.0 121.0 all-gather.10
  461.2 114.6 all-gather.14
  577.8 114.5 all-gather.16
